TPU v7x, 128 devices: a whole 4x4x4 slice. The times are simulated.
128 devices in a mesh: dp: 8 (over x, core), pair: 16 (over z, y).
Axes of the slice: x: 4, y: 4, z: 4, core: 2. Of those that a mesh axis runs over, the one named last changes fastest.
Arguments:
- anchor: bfloat16 [5, 4096, 1024], P(None, ('dp', 'pair')), may hold values from -20 to 20
- partner: bfloat16 [5, 4096, 1024], P(None, ('dp', 'pair')), may hold values from -12 to 12
- counts: int32 [5], replicated, may hold values from 512 to 4096, as said below
- pair_scale: float32 [5], replicated, may hold values from 2 to 8
Outputs:
- loss_value: float32 [], replicated
- grad_anchor: float32 [5, 4096, 1024], P(None, ('dp', 'pair'))
- grad_partner: float32 [5, 4096, 1024], P(None, ('dp', 'pair'))
Inputs may be any that keep to these rules, and one draw needn't show every extreme that they name: The valid samples of pair p are its rows 0 to counts[p] - 1; one pair has all 4096 rows valid.
All inputs are finite; a program needn't handle non-finite values.
Results may differ from a plain program's by a relative error of at most 0.0021.
Values may be sent and summed in bfloat16 or wider, within the bound.
No kernel may reach another device: no remote copies, remote signals or barrier semaphores. Data moves between devices by JAX's collectives and lax.ppermute only.
A program may use at most 128 MiB of HBM per device.

v0:
```python
import math
import jax
import jax.numpy as jnp
from jax import lax
from jax.sharding import PartitionSpec as P

NEG = -1e30


def merge_gathered(stats):
    highs = stats[:, 0]
    sums = stats[:, 1]
    highest = jnp.max(highs, axis=0)
    summed = jnp.sum(sums * jnp.exp(highs - highest[None]), axis=0)
    return (highest, summed)


def per_device(anchor, partner, counts, pair_scale):
    pair_count, shard_rows, model_width = anchor.shape
    score_scale = 4.0 / math.sqrt(model_width)
    dp_size = lax.axis_size("dp")
    pair_size = lax.axis_size("pair")
    dp_index = lax.axis_index("dp")
    pair_place = lax.axis_index("pair")
    own_first = (dp_index * pair_size + pair_place) * shard_rows
    row_set = lax.all_gather(anchor, "pair", axis=1, tiled=True)
    col_set = lax.all_gather(partner, "dp", axis=1, tiled=True)
    row_count = row_set.shape[1]
    offsets = jnp.arange(shard_rows, dtype=jnp.int32)
    row_global = dp_index * row_count + jnp.arange(row_count, dtype=jnp.int32)
    col_first = (jnp.arange(dp_size, dtype=jnp.int32) * pair_size + pair_place) * shard_rows
    col_global = (col_first[:, None] + offsets[None, :]).reshape(-1)
    row_valid = row_global[None, :] < counts[:, None]
    col_valid = col_global[None, :] < counts[:, None]
    inside = row_valid[:, :, None] & col_valid[:, None, :]
    scores = (
        jnp.einsum("prd,pcd->prc", row_set, col_set, preferred_element_type=jnp.float32)
        * score_scale
    )
    masked = jnp.where(inside, scores, NEG)
    row_high = jnp.max(masked, axis=2)
    row_sum = jnp.sum(jnp.where(inside, jnp.exp(masked - row_high[:, :, None]), 0.0), axis=2)
    col_high = jnp.max(masked, axis=1)
    col_sum = jnp.sum(jnp.where(inside, jnp.exp(masked - col_high[:, None, :]), 0.0), axis=1)
    row_stats = lax.all_gather(jnp.stack([row_high, row_sum]), "pair")
    col_stats = lax.all_gather(jnp.stack([col_high, col_sum]), "dp")
    row_high, row_sum = merge_gathered(row_stats)
    col_high, col_sum = merge_gathered(col_stats)
    row_lse = jnp.where(row_valid, row_high + jnp.log(jnp.where(row_valid, row_sum, 1.0)), 0.0)
    col_lse = jnp.where(col_valid, col_high + jnp.log(jnp.where(col_valid, col_sum, 1.0)), 0.0)
    own_valid = own_first + offsets[None, :] < counts[:, None]
    row_own = lax.dynamic_slice_in_dim(row_lse, pair_place * shard_rows, shard_rows, 1)
    col_own = lax.dynamic_slice_in_dim(col_lse, dp_index * shard_rows, shard_rows, 1)
    positive = (
        jnp.sum(anchor.astype(jnp.float32) * partner.astype(jnp.float32), axis=2) * score_scale
    )
    loss_terms = jnp.where(own_valid, row_own + col_own - 2.0 * positive, 0.0)
    totals = lax.psum(jnp.sum(loss_terms, axis=1), ("dp", "pair"))
    loss_value = jnp.sum(totals / (2.0 * counts.astype(jnp.float32))) / pair_count
    prob_row = jnp.where(inside, jnp.exp(scores - row_lse[:, :, None]), 0.0)
    prob_col = jnp.where(inside, jnp.exp(scores - col_lse[:, None, :]), 0.0)
    weights = (pair_scale[:, None, None] * 0.5 * (prob_row + prob_col)).astype(jnp.bfloat16)
    grad_rows = (
        jnp.einsum("prc,pcd->prd", weights, col_set, preferred_element_type=jnp.float32)
        * score_scale
    )
    grad_cols = (
        jnp.einsum("prc,prd->pcd", weights, row_set, preferred_element_type=jnp.float32)
        * score_scale
    )
    anchor_part = lax.psum_scatter(grad_rows, "pair", scatter_dimension=1, tiled=True)
    partner_part = lax.psum_scatter(grad_cols, "dp", scatter_dimension=1, tiled=True)
    own_term = (pair_scale * score_scale)[:, None, None]
    keep_rows = own_valid[:, :, None]
    anchor_out = jnp.where(keep_rows, anchor_part - own_term * partner.astype(jnp.float32), 0.0)
    partner_out = jnp.where(keep_rows, partner_part - own_term * anchor.astype(jnp.float32), 0.0)
    return (loss_value, anchor_out, partner_out)


def solution(mesh):
    in_specs = (P(None, ("dp", "pair"), None), P(None, ("dp", "pair"), None), P(), P())
    out_specs = (P(), P(None, ("dp", "pair"), None), P(None, ("dp", "pair"), None))
    return jax.shard_map(
        per_device, mesh=mesh, in_specs=in_specs, out_specs=out_specs, check_vma=False
    )
```

profile of v0, /device:TPU:1, one launch (start us, length us, event | category | flops | bytes accessed | tf_op | source)
XLA Modules:
  0.0 354.5 jit_solution(2730051306671288347)
XLA Ops:
  7.2 0.0 all-gather.7.cloned.1.call-start
  7.2 0.7 all-gather.7.cloned.1.call-update
  7.9 0.0 all-gather.5.cloned.1.call-start
  7.9 0.7 all-gather.5.cloned.1.call-update
  8.6 0.0 reduce-scatter.5.cloned.1.call-start
  8.7 0.1 iota_add_fusion
  8.8 0.1 add.96
  8.9 0.7 broadcast_multiply_fusion.2
  9.5 0.7 broadcast_compare_fusion.1
  10.3 0.7 broadcast_compare_fusion
  11.0 28.5 %all-gather.7.cloned.1.call-done = bf16[5,256,1024]{2,1,0:T(8,128)(2,1)} async-done(((bf16[5,32,1024]{2,1,0:T(8,128)(2,1)}), bf16[5,256,1024]{2,1,0:T(8,128)(2,1)}) %all-gather.7.cloned.1.call-update) | async-done | bytes 2621456 | tf_op jit(solution)/shard_map/all_gather | solution.py:27
  39.4 58.8 %all-gather.5.cloned.1.call-done = bf16[5,512,1024]{2,1,0:T(8,128)(2,1)} async-done(((bf16[5,32,1024]{2,1,0:T(8,128)(2,1)}), bf16[5,512,1024]{2,1,0:T(8,128)(2,1)}) %all-gather.5.cloned.1.call-update) | async-done | bytes 5242896 | tf_op jit(solution)/shard_map/all_gather | solution.py:26
  98.2 4.9 %fusion.6 = (f32[5,512]{1,0:T(8,128)S(1)}, f32[5,256]{1,0:T(8,128)S(1)}, f32[5,512,256]{2,1,0:T(8,128)S(1)}) fusion(pred[5,256]{1,0:T(8,128)(4,1)S(1)} %broadcast_compare_fusion.1, pred[5,512]{1,0:T(8,128)(4,1)S(1)} %broadcast_compare_fusion, bf16[5,512,1024]{2,1,0:T(8,128)(2,1)} %all-gather.5.cloned.1.call-done, ...), kind=kOutput, calls=%fused_computation.13 | convolution fusion | flops 1345450240 | bytes 10504960 | tf_op jit(solution)/shard_map/prd,pcd->prc/dot_general | solution.py:37
  103.2 0.0 copy-start.2
  103.2 2.0 fusion
  105.2 13.6 %all-gather.1 = f32[16,5,256]{2,1,0:T(8,128)S(1)} all-gather(f32[2,5,256]{2,1,0:T(8,128)S(1)} %pad_maximum_fusion.1), channel_id=3, replica_groups=mesh['dp'=8,'pair'=16] {'dp'}, dimensions={0}, use_global_device_ids=true | all-gather | bytes 92160 | tf_op jit(solution)/shard_map/all_gather | solution.py:46
  118.9 0.1 add_select_fusion.1
  119.0 18.7 %all-gather = f32[32,5,512]{2,1,0:T(8,128)S(1)} all-gather(f32[2,5,512]{2,1,0:T(8,128)S(1)} %pad_maximum_fusion), channel_id=2, replica_groups=mesh['dp'=8,'pair'=16] {'pair'}, dimensions={0}, use_global_device_ids=true | all-gather | bytes 348160 | tf_op jit(solution)/shard_map/all_gather | solution.py:45
  137.7 0.1 fusion.13
  137.8 0.1 add_select_fusion
  137.8 5.1 %broadcast_multiply_fusion.1 = f32[5,256,1024]{2,1,0:T(8,128)} fusion(bf16[5,512,1024]{2,1,0:T(8,128)(2,1)S(1)} %copy-done.3, f32[5,512,256]{2,1,0:T(8,128)S(1)} %get-tuple-element.12, f32[5,256]{1,0:T(8,128)S(1)} %add_select_fusion.1, f32[5,512]{1,0:T(8,128)S(1)} %add_select_fusion, f32[5]{0:T(128)S(1)} %get-tuple-element.11, ...), kind=kOutput, calls=%fused_computation.11 | convolution fusion | flops 1349386240 | bytes 13126420 | tf_op jit(solution)/shard_map/prc,prd->pcd/dot_general | solution.py:68
  142.9 0.0 reduce-scatter.5.cloned.1.call-update
  142.9 0.0 reduce-scatter.3.cloned.1.call-start
  143.0 7.6 %broadcast_multiply_fusion = f32[5,512,1024]{2,1,0:T(8,128)} fusion(bf16[5,256,1024]{2,1,0:T(8,128)(2,1)} %all-gather.7.cloned.1.call-done, f32[5,512,256]{2,1,0:T(8,128)S(1)} %get-tuple-element.12, f32[5,256]{1,0:T(8,128)S(1)} %add_select_fusion.1, f32[5,512]{1,0:T(8,128)S(1)} %add_select_fusion, f32[5]{0:T(128)S(1)} %get-tuple-element.11, ...), kind=kOutput, calls=%fused_computation.5 | convolution fusion | flops 1350696960 | bytes 15747860 | tf_op jit(solution)/shard_map/prc,pcd->prd/dot_general | solution.py:64
  150.6 0.0 reduce-scatter.3.cloned.1.call-update
  150.6 0.1 broadcast_compare_fusion.2
  150.7 32.2 %reduce-scatter.5.cloned.1.call-done = f32[5,32,1024]{2,1,0:T(8,128)} async-done(((f32[5,256,1024]{2,1,0:T(8,128)}), f32[5,32,1024]{2,1,0:T(8,128)}) %reduce-scatter.5.cloned.1.call-update) | async-done | bytes 655376 | tf_op jit(solution)/shard_map/reduce_scatter | solution.py:72
  182.9 94.8 %reduce-scatter.3.cloned.1.call-done = f32[5,32,1024]{2,1,0:T(8,128)} async-done(((f32[5,512,1024]{2,1,0:T(8,128)}), f32[5,32,1024]{2,1,0:T(8,128)}) %reduce-scatter.3.cloned.1.call-update) | async-done | bytes 655376 | tf_op jit(solution)/shard_map/reduce_scatter | solution.py:71
  277.7 2.7 fusion.8
  280.4 0.2 select_reduce_fusion
  280.6 65.0 %psum.7 = f32[5]{0:T(128)S(1)} all-reduce(f32[5]{0:T(128)S(1)} %select_reduce_fusion), channel_id=1, replica_groups=mesh['dp'=8,'pair'=16] {'dp','pair'}, use_global_device_ids=true, to_apply=%region_10.11 | all-reduce | flops 5 | bytes 40 | tf_op jit(solution)/shard_map/psum | solution.py:58
  345.6 0.6 fusion.18
  (15 shorter events, 0.1 us)
Async XLA Ops:
  7.2 32.3 %all-gather.7.cloned.1.call-start = ((), (), s32[]{:S(2)}) async-start(), calls=%async_computation.3 | async-start | bytes 2949120 | tf_op jit(solution)/shard_map/all_gather | solution.py:27
  7.9 90.3 %all-gather.5.cloned.1.call-start = ((), (), s32[]{:S(2)}) async-start(), calls=%async_computation.2 | async-start | bytes 5570560 | tf_op jit(solution)/shard_map/all_gather | solution.py:26
  8.6 174.2 %reduce-scatter.5.cloned.1.call-start = ((), (), s32[]{:S(2)}) async-start(), calls=%async_computation.5 | async-start | bytes 5898240 | tf_op jit(solution)/shard_map/reduce_scatter | solution.py:72
  98.2 39.6 %copy-start.3 = (bf16[5,512,1024]{2,1,0:T(8,128)(2,1)S(1)}, bf16[5,512,1024]{2,1,0:T(8,128)(2,1)}, u32[]{:S(2)}) copy-start(bf16[5,512,1024]{2,1,0:T(8,128)(2,1)} %all-gather.5.cloned.1.call-done) | copy-start | bytes 15728644
  103.2 15.7 %copy-start.2 = (s32[5]{0:T(128)S(1)}, s32[5]{0:T(128)}, u32[]{:S(2)}) copy-start(s32[5]{0:T(128)} %param.6) | copy-start | bytes 64
  142.9 134.8 %reduce-scatter.3.cloned.1.call-start = ((), (), s32[]{:S(2)}) async-start(), calls=%async_computation.4 | async-start | bytes 11141120 | tf_op jit(solution)/shard_map/reduce_scatter | solution.py:71
  150.5 127.1 %copy-start = (bf16[5,32,1024]{2,1,0:T(8,128)(2,1)S(1)}, bf16[5,32,1024]{2,1,0:T(8,128)(2,1)}, u32[]{:S(2)}) copy-start(bf16[5,32,1024]{2,1,0:T(8,128)(2,1)} %param.5) | copy-start | bytes 983044
  150.5 127.1 %copy-start.1 = (bf16[5,32,1024]{2,1,0:T(8,128)(2,1)S(1)}, bf16[5,32,1024]{2,1,0:T(8,128)(2,1)}, u32[]{:S(2)}) copy-start(bf16[5,32,1024]{2,1,0:T(8,128)(2,1)} %param.4) | copy-start | bytes 983044
Sparse Core Ops, SparseCore 0:
  9.7 29.7 all-gather.6
  41.6 56.6 all-gather.4
  143.0 39.7 reduce-scatter.4
  186.2 91.4 reduce-scatter.2
where the time goes:
time: 355 us
  waiting for transfers between devices  216 us (61%)
  blocking collectives  97.3 us (27%)
  matrix products  17.6 us (5%)
  between operations  15.6 us (4%)
  other arithmetic  8.11 us (2%)
    reduce_scatter x1, waiting for transfers between devices, per_device(): lax.psum_scatter(grad_rows, 'pair', scatter_dimension=1, tiled=True)  94.8 us
    psum x1, blocking collectives, per_device(): totals = lax.psum(jnp.sum(loss_terms, axis=1), ('dp', 'pair'))  65 us
    all_gather x1, waiting for transfers between devices, per_device(): row_set = lax.all_gather(anchor, 'pair', axis=1, tiled=True)  58.8 us
    reduce_scatter x1, waiting for transfers between devices, per_device(): lax.psum_scatter(grad_cols, 'dp', scatter_dimension=1, tiled=True)  32.2 us
    all_gather x1, waiting for transfers between devices, per_device(): col_set = lax.all_gather(partner, 'dp', axis=1, tiled=True)  28.5 us
    all_gather x1, blocking collectives, per_device(): row_stats = lax.all_gather(jnp.stack([row_high, row_sum]), 'pair')  18.7 us
    all_gather x1, blocking collectives, per_device(): col_stats = lax.all_gather(jnp.stack([col_high, col_sum]), 'dp')  13.6 us
    dot_general x1, matrix products, per_device(): jnp.einsum('prc,pcd->prd', weights, col_set, preferred_element_type=jnp.f...  7.57 us
  transfers between devices with their start and end apart: 4, of which 4 were waited for; matrix products, arithmetic and copies ran while one was open for 3% of the time, Pallas kernels for 0%

commit v1 on v0

--- a/solution.py
+++ b/solution.py
@@ -24,7 +24,20 @@
     pair_place = lax.axis_index("pair")
     own_first = (dp_index * pair_size + pair_place) * shard_rows
     row_set = lax.all_gather(anchor, "pair", axis=1, tiled=True)
-    col_set = lax.all_gather(partner, "dp", axis=1, tiled=True)
+
+    def wait_arrays(local_x):
+        amount_of = lax.axis_size("dp")
+        pool = [local_x]
+        for j in [*range(amount_of - 1)]:
+            front = lax.ppermute(
+                pool[-1], axis_name="dp", perm=[(i, (i + 1) % amount_of) for i in range(amount_of)]
+            )
+            pool.append(front)
+        ready = jnp.concatenate(pool[::-1], axis=1)
+        near = lax.axis_index("dp")
+        return jnp.roll(ready, shift=(near + 1) * local_x.shape[1], axis=1)
+
+    col_set = wait_arrays(partner)
     row_count = row_set.shape[1]
     offsets = jnp.arange(shard_rows, dtype=jnp.int32)
     row_global = dp_index * row_count + jnp.arange(row_count, dtype=jnp.int32)

time: 355 us -> 334 us (0.941)
  waiting for transfers between devices: 216 us -> 159 us
  starting transfers between devices: 0.16 us -> 14.8 us
  local copies, waits for them, and re-layouts: 0.1 us -> 13.1 us
  blocking collectives: 97.3 us -> 105 us
    all_gather x1, waiting for transfers between devices: 58.8 us -> 0.01 us  [per_device(): row_set = lax.all_gather(anchor, 'pair', axis=1, tiled=True)]
    ppermute x0 -> x7, waiting for transfers between devices: none -> 32.1 us  [wait_arrays(): lax.ppermute(pool[-1], axis_name='dp', perm=[(i, (i + 1) % amount_of) for...]
    all_gather x1 -> x0, waiting for transfers between devices: 28.5 us -> none  [per_device(): col_set = lax.all_gather(partner, 'dp', axis=1, tiled=True)]
    ppermute x0 -> x7, starting transfers between devices: none -> 14.6 us  [wait_arrays(): lax.ppermute(pool[-1], axis_name='dp', perm=[(i, (i + 1) % amount_of) for...]
    unnamed x8 -> x23, local copies, waits for them, and re-layouts: 0.02 us -> 12.3 us
    all_gather x1, blocking collectives: 13.6 us -> 19.2 us  [per_device(): col_stats = lax.all_gather(jnp.stack([col_high, col_sum]), 'dp')]
  transfers between devices with their start and end apart: 4 -> 10, of which waited for: 4 -> 9; matrix products, arithmetic and copies ran while one was open for 3% -> 7% of each run, Pallas kernels for 0% -> 0%
where the time goes in v1:
time: 334 us
  waiting for transfers between devices  159 us (48%)
  blocking collectives  105 us (31%)
  matrix products  18.7 us (6%)
  between operations  15.6 us (5%)
  starting transfers between devices  14.8 us (4%)
  local copies, waits for them, and re-layouts  13.1 us (4%)
  other arithmetic  8 us (2%)
    reduce_scatter x1, waiting for transfers between devices, per_device(): lax.psum_scatter(grad_rows, 'pair', scatter_dimension=1, tiled=True)  94.8 us
    psum x1, blocking collectives, per_device(): totals = lax.psum(jnp.sum(loss_terms, axis=1), ('dp', 'pair'))  65.1 us
    ppermute x7, waiting for transfers between devices, wait_arrays(): lax.ppermute(pool[-1], axis_name='dp', perm=[(i, (i + 1) % amount_of) for...  32.1 us
    reduce_scatter x1, waiting for transfers between devices, per_device(): lax.psum_scatter(grad_cols, 'dp', scatter_dimension=1, tiled=True)  31.4 us
    all_gather x1, blocking collectives, per_device(): row_stats = lax.all_gather(jnp.stack([row_high, row_sum]), 'pair')  20.4 us
    all_gather x1, blocking collectives, per_device(): col_stats = lax.all_gather(jnp.stack([col_high, col_sum]), 'dp')  19.2 us
    ppermute x7, starting transfers between devices, wait_arrays(): lax.ppermute(pool[-1], axis_name='dp', perm=[(i, (i + 1) % amount_of) for...  14.6 us
    unnamed x23, local copies, waits for them, and re-layouts  12.3 us
  transfers between devices with their start and end apart: 10, of which 9 were waited for; matrix products, arithmetic and copies ran while one was open for 7% of the time, Pallas kernels for 0%

profile of v1, /device:TPU:1, one launch (start us, length us, event | category | flops | bytes accessed | tf_op | source)
XLA Modules:
  0.0 333.8 jit_solution(8632040423517312908)
XLA Ops:
  8.0 2.6 collective-permute-start
  10.6 4.3 %collective-permute-done = bf16[5,32,1024]{2,1,0:T(8,128)(2,1)S(1)} collective-permute-done((bf16[5,32,1024]{2,1,0:T(8,128)(2,1)}, bf16[5,32,1024]{2,1,0:T(8,128)(2,1)S(1)}, u32[]{:S(2)}, u32[]{:S(2)}) %collective-permute-start) | collective-permute-done | bytes 327712 | tf_op jit(solution)/shard_map/ppermute | solution.py:32
  14.9 2.4 collective-permute-start.1
  17.3 4.0 %collective-permute-done.1 = bf16[5,32,1024]{2,1,0:T(8,128)(2,1)S(1)} collective-permute-done((bf16[5,32,1024]{2,1,0:T(8,128)(2,1)S(1)}, bf16[5,32,1024]{2,1,0:T(8,128)(2,1)S(1)}, u32[]{:S(2)}, u32[]{:S(2)}) %collective-permute-start.1) | collective-permute-done | bytes 327712 | tf_op jit(solution)/shard_map/ppermute | solution.py:32
  21.3 2.5 collective-permute-start.2
  23.8 4.0 %collective-permute-done.2 = bf16[5,32,1024]{2,1,0:T(8,128)(2,1)S(1)} collective-permute-done((bf16[5,32,1024]{2,1,0:T(8,128)(2,1)S(1)}, bf16[5,32,1024]{2,1,0:T(8,128)(2,1)S(1)}, u32[]{:S(2)}, u32[]{:S(2)}) %collective-permute-start.2) | collective-permute-done | bytes 327712 | tf_op jit(solution)/shard_map/ppermute | solution.py:32
  27.8 2.5 collective-permute-start.3
  30.3 4.0 %collective-permute-done.3 = bf16[5,32,1024]{2,1,0:T(8,128)(2,1)S(1)} collective-permute-done((bf16[5,32,1024]{2,1,0:T(8,128)(2,1)S(1)}, bf16[5,32,1024]{2,1,0:T(8,128)(2,1)S(1)}, u32[]{:S(2)}, u32[]{:S(2)}) %collective-permute-start.3) | collective-permute-done | bytes 327712 | tf_op jit(solution)/shard_map/ppermute | solution.py:32
  34.3 2.5 collective-permute-start.4
  36.9 4.7 %collective-permute-done.4 = bf16[5,32,1024]{2,1,0:T(8,128)(2,1)S(1)} collective-permute-done((bf16[5,32,1024]{2,1,0:T(8,128)(2,1)S(1)}, bf16[5,32,1024]{2,1,0:T(8,128)(2,1)S(1)}, u32[]{:S(2)}, u32[]{:S(2)}) %collective-permute-start.4) | collective-permute-done | bytes 327712 | tf_op jit(solution)/shard_map/ppermute | solution.py:32
  41.6 1.7 collective-permute-start.5
  44.7 4.5 %collective-permute-done.5 = bf16[5,32,1024]{2,1,0:T(8,128)(2,1)S(1)} collective-permute-done((bf16[5,32,1024]{2,1,0:T(8,128)(2,1)S(1)}, bf16[5,32,1024]{2,1,0:T(8,128)(2,1)S(1)}, u32[]{:S(2)}, u32[]{:S(2)}) %collective-permute-start.5) | collective-permute-done | bytes 327712 | tf_op jit(solution)/shard_map/ppermute | solution.py:32
  50.5 6.5 %collective-permute-done.6 = bf16[5,32,1024]{2,1,0:T(8,128)(2,1)S(1)} collective-permute-done((bf16[5,32,1024]{2,1,0:T(8,128)(2,1)S(1)}, bf16[5,32,1024]{2,1,0:T(8,128)(2,1)S(1)}, u32[]{:S(2)}, u32[]{:S(2)}) %collective-permute-start.6) | collective-permute-done | bytes 327712 | tf_op jit(solution)/shard_map/ppermute | solution.py:32
  57.0 0.8 constant_dynamic-update-slice_fusion.15
  59.2 0.8 constant_dynamic-update-slice_fusion.12
  60.7 0.8 constant_dynamic-update-slice_fusion.10
  62.2 1.7 constant_dynamic-update-slice_fusion.8
  65.4 0.8 constant_dynamic-update-slice_fusion.5
  66.2 0.8 constant_dynamic-update-slice_fusion.4
  67.0 0.8 constant_dynamic-update-slice_fusion.3
  67.7 0.8 constant_dynamic-update-slice_fusion.2
  69.2 0.8 constant_dynamic-update-slice_fusion
  70.0 5.3 %fusion.11 = (f32[5,512]{1,0:T(8,128)S(1)}, f32[5,256]{1,0:T(8,128)S(1)}, f32[5,256,512]{2,1,0:T(8,128)S(1)}) fusion(pred[5,256]{1,0:T(8,128)(4,1)S(1)} %broadcast_compare_fusion.1, pred[5,512]{1,0:T(8,128)(4,1)S(1)} %broadcast_compare_fusion, bf16[5,512,1024]{2,1,0:T(8,128)(2,1)} %all-gather.4.cloned.1.call-done, ...), kind=kOutput, calls=%fused_computation.20 | convolution fusion | flops 1345450240 | bytes 10504964 | tf_op jit(solution)/shard_map/prd,pcd->prc/dot_general | solution.py:50
  75.4 1.9 fusion
  77.3 19.2 %all-gather.1 = f32[16,5,256]{2,1,0:T(8,128)S(1)} all-gather(f32[2,5,256]{2,1,0:T(8,128)S(1)} %pad_maximum_fusion.1), channel_id=3, replica_groups=mesh['dp'=8,'pair'=16] {'dp'}, dimensions={0}, use_global_device_ids=true | all-gather | bytes 92160 | tf_op jit(solution)/shard_map/all_gather | solution.py:59
  96.6 20.4 %all-gather = f32[32,5,512]{2,1,0:T(8,128)S(1)} all-gather(f32[2,5,512]{2,1,0:T(8,128)S(1)} %pad_maximum_fusion), channel_id=2, replica_groups=mesh['dp'=8,'pair'=16] {'pair'}, dimensions={0}, use_global_device_ids=true | all-gather | bytes 348160 | tf_op jit(solution)/shard_map/all_gather | solution.py:58
  117.2 5.1 %broadcast_multiply_fusion.1 = f32[5,256,1024]{2,1,0:T(8,128)} fusion(bf16[5,512,1024]{2,1,0:T(8,128)(2,1)S(1)} %copy-done.3, f32[5,256,512]{2,1,0:T(8,128)S(1)} %get-tuple-element.12, f32[5,256]{1,0:T(8,128)S(1)} %add_select_fusion.1, f32[5,512]{1,0:T(8,128)S(1)} %add_select_fusion, f32[5]{0:T(128)S(1)} %get-tuple-element.11, ...), kind=kOutput, calls=%fused_computation.15 | convolution fusion | flops 1349386240 | bytes 13126420 | tf_op jit(solution)/shard_map/prc,prd->pcd/dot_general | solution.py:81
  122.4 8.3 %broadcast_multiply_fusion = f32[5,512,1024]{2,1,0:T(8,128)} fusion(bf16[5,512,1024]{2,1,0:T(8,128)(2,1)} %constant_dynamic-update-slice_fusion, s32[]{:T(128)S(6)} %select_n.77, f32[5,256,512]{2,1,0:T(8,128)S(1)} %get-tuple-element.12, f32[5,256]{1,0:T(8,128)S(1)} %add_select_fusion.1, f32[5,512]{1,0:T(8,128)S(1)} %add_select_fusion, ...), kind=kOutput, calls=%fused_computation.5 | convolution fusion | flops 1350696960 | bytes 15747864 | tf_op jit(solution)/shard_map/prc,pcd->prd/dot_general | solution.py:77
  130.7 31.4 %reduce-scatter.5.cloned.1.call-done = f32[5,32,1024]{2,1,0:T(8,128)} async-done(((f32[5,256,1024]{2,1,0:T(8,128)}), f32[5,32,1024]{2,1,0:T(8,128)}) %reduce-scatter.5.cloned.1.call-update) | async-done | bytes 655376 | tf_op jit(solution)/shard_map/reduce_scatter | solution.py:85
  162.1 94.8 %reduce-scatter.3.cloned.1.call-done = f32[5,32,1024]{2,1,0:T(8,128)} async-done(((f32[5,512,1024]{2,1,0:T(8,128)}), f32[5,32,1024]{2,1,0:T(8,128)}) %reduce-scatter.3.cloned.1.call-update) | async-done | bytes 655376 | tf_op jit(solution)/shard_map/reduce_scatter | solution.py:84
  256.9 2.7 fusion.13
  259.8 65.1 %psum.7 = f32[5]{0:T(128)S(1)} all-reduce(f32[5]{0:T(128)S(1)} %select_reduce_fusion), channel_id=1, replica_groups=mesh['dp'=8,'pair'=16] {'dp','pair'}, use_global_device_ids=true, to_apply=%region_10.11 | all-reduce | flops 5 | bytes 40 | tf_op jit(solution)/shard_map/psum | solution.py:71
  (42 shorter events, 10.0 us)
Async XLA Ops:
  7.2 62.1 %copy-start = (bf16[5,32,1024]{2,1,0:T(8,128)(2,1)S(1)}, bf16[5,32,1024]{2,1,0:T(8,128)(2,1)}, u32[]{:S(2)}) copy-start(bf16[5,32,1024]{2,1,0:T(8,128)(2,1)} %param.5) | copy-start | bytes 983044
  7.2 62.8 %all-gather.4.cloned.1.call-start = ((), (), s32[]{:S(2)}) async-start(), calls=%async_computation.2 | async-start | bytes 5570560 | tf_op jit(solution)/shard_map/all_gather | solution.py:26
  7.9 154.2 %reduce-scatter.5.cloned.1.call-start = ((), (), s32[]{:S(2)}) async-start(), calls=%async_computation.4 | async-start | bytes 5898240 | tf_op jit(solution)/shard_map/reduce_scatter | solution.py:85
  8.0 6.9 %collective-permute-start = (bf16[5,32,1024]{2,1,0:T(8,128)(2,1)}, bf16[5,32,1024]{2,1,0:T(8,128)(2,1)S(1)}, u32[]{:S(2)}, u32[]{:S(2)}) collective-permute-start(bf16[5,32,1024]{2,1,0:T(8,128)(2,1)} %param.5), channel_id=1, source_target_pairs={{0,16},{16,32},{32,48},{48,64},{64,80},{80,96},{96,112},{112,0},{1... | collective-permute-start | bytes 983048 | tf_op jit(solution)/shard_map/ppermute | solution.py:32
  14.9 6.4 %collective-permute-start.1 = (bf16[5,32,1024]{2,1,0:T(8,128)(2,1)S(1)}, bf16[5,32,1024]{2,1,0:T(8,128)(2,1)S(1)}, u32[]{:S(2)}, u32[]{:S(2)}) collective-permute-start(bf16[5,32,1024]{2,1,0:T(8,128)(2,1)S(1)} %collective-permute-done), channel_id=1, source_target_pairs={{0,16},{16,32},{32,48},{48,64},{64,80},{80,96},{96,112},{112,0},{1... | collective-permute-start | bytes 983048 | tf_op jit(solution)/shard_map/ppermute | solution.py:32
  21.3 6.5 %collective-permute-start.2 = (bf16[5,32,1024]{2,1,0:T(8,128)(2,1)S(1)}, bf16[5,32,1024]{2,1,0:T(8,128)(2,1)S(1)}, u32[]{:S(2)}, u32[]{:S(2)}) collective-permute-start(bf16[5,32,1024]{2,1,0:T(8,128)(2,1)S(1)} %collective-permute-done.1), channel_id=1, source_target_pairs={{0,16},{16,32},{32,48},{48,64},{64,80},{80,96},{96,112},{112,0},{1... | collective-permute-start | bytes 983048 | tf_op jit(solution)/shard_map/ppermute | solution.py:32
  27.8 6.5 %collective-permute-start.3 = (bf16[5,32,1024]{2,1,0:T(8,128)(2,1)S(1)}, bf16[5,32,1024]{2,1,0:T(8,128)(2,1)S(1)}, u32[]{:S(2)}, u32[]{:S(2)}) collective-permute-start(bf16[5,32,1024]{2,1,0:T(8,128)(2,1)S(1)} %collective-permute-done.2), channel_id=1, source_target_pairs={{0,16},{16,32},{32,48},{48,64},{64,80},{80,96},{96,112},{112,0},{1... | collective-permute-start | bytes 983048 | tf_op jit(solution)/shard_map/ppermute | solution.py:32
  34.3 7.3 %collective-permute-start.4 = (bf16[5,32,1024]{2,1,0:T(8,128)(2,1)S(1)}, bf16[5,32,1024]{2,1,0:T(8,128)(2,1)S(1)}, u32[]{:S(2)}, u32[]{:S(2)}) collective-permute-start(bf16[5,32,1024]{2,1,0:T(8,128)(2,1)S(1)} %collective-permute-done.3), channel_id=1, source_target_pairs={{0,16},{16,32},{32,48},{48,64},{64,80},{80,96},{96,112},{112,0},{1... | collective-permute-start | bytes 983048 | tf_op jit(solution)/shard_map/ppermute | solution.py:32
  41.6 7.7 %collective-permute-start.5 = (bf16[5,32,1024]{2,1,0:T(8,128)(2,1)S(1)}, bf16[5,32,1024]{2,1,0:T(8,128)(2,1)S(1)}, u32[]{:S(2)}, u32[]{:S(2)}) collective-permute-start(bf16[5,32,1024]{2,1,0:T(8,128)(2,1)S(1)} %collective-permute-done.4), channel_id=1, source_target_pairs={{0,16},{16,32},{32,48},{48,64},{64,80},{80,96},{96,112},{112,0},{1... | collective-permute-start | bytes 983048 | tf_op jit(solution)/shard_map/ppermute | solution.py:32
  49.3 7.7 %collective-permute-start.6 = (bf16[5,32,1024]{2,1,0:T(8,128)(2,1)S(1)}, bf16[5,32,1024]{2,1,0:T(8,128)(2,1)S(1)}, u32[]{:S(2)}, u32[]{:S(2)}) collective-permute-start(bf16[5,32,1024]{2,1,0:T(8,128)(2,1)S(1)} %collective-permute-done.5), channel_id=1, source_target_pairs={{0,16},{16,32},{32,48},{48,64},{64,80},{80,96},{96,112},{112,0},{1... | collective-permute-start | bytes 983048 | tf_op jit(solution)/shard_map/ppermute | solution.py:32
  70.0 26.5 %copy-start.2 = (s32[5]{0:T(128)S(1)}, s32[5]{0:T(128)}, u32[]{:S(2)}) copy-start(s32[5]{0:T(128)} %param.6) | copy-start | bytes 64
  70.0 47.2 %copy-start.3 = (bf16[5,512,1024]{2,1,0:T(8,128)(2,1)S(1)}, bf16[5,512,1024]{2,1,0:T(8,128)(2,1)}, u32[]{:S(2)}) copy-start(bf16[5,512,1024]{2,1,0:T(8,128)(2,1)} %all-gather.4.cloned.1.call-done) | copy-start | bytes 15728644
  122.3 134.6 %reduce-scatter.3.cloned.1.call-start = ((), (), s32[]{:S(2)}) async-start(), calls=%async_computation.3 | async-start | bytes 11141120 | tf_op jit(solution)/shard_map/reduce_scatter | solution.py:84
  130.6 126.3 %copy-start.1 = (bf16[5,32,1024]{2,1,0:T(8,128)(2,1)S(1)}, bf16[5,32,1024]{2,1,0:T(8,128)(2,1)}, u32[]{:S(2)}) copy-start(bf16[5,32,1024]{2,1,0:T(8,128)(2,1)} %param.4) | copy-start | bytes 983044
Sparse Core Ops, SparseCore 0:
  10.2 59.6 all-gather.3
  122.4 39.6 reduce-scatter.4
  165.6 91.3 reduce-scatter.2
